TPU v7x, 512 devices: a whole 4x8x8 slice. The times are simulated.
512 devices in a mesh: dp: 8 (over z), expert: 16 (over y, core), etp: 4 (over x).
Axes of the slice: x: 4, y: 8, z: 8, core: 2. Of those that a mesh axis runs over, the one named last changes fastest.
Arguments:
- tokens: bfloat16 [3072, 4096], P(('dp', 'expert')), may hold values from -6 to 6
- cotangent: bfloat16 [3072, 4096], P(('dp', 'expert')), may hold values from -3 to 3
- route_weights: float32 [3072, 8], P(('dp', 'expert')), may hold values from 0.05 to 0.3
- expert_ids: int32 [3072, 8], P(('dp', 'expert')), may hold values from 0 to 15, as said below
- w_gate: bfloat16 [16, 1536, 4096], P('expert', 'etp', 'dp'), may hold values from -0.09375 to 0.09375
- w_up: bfloat16 [16, 1536, 4096], P('expert', 'etp', 'dp'), may hold values from -0.09375 to 0.09375
- w_down: bfloat16 [16, 1536, 4096], P('expert', 'etp', 'dp'), may hold values from -0.15625 to 0.15625
Outputs:
- mixed: bfloat16 [3072, 4096], P(('dp', 'expert'), 'etp')
- grad_tokens: bfloat16 [3072, 4096], P(('dp', 'expert'), 'etp')
- grad_gate: float32 [16, 1536, 4096], P('expert', 'etp', 'dp')
Inputs may be any that keep to these rules, and one draw needn't show every extreme that they name: `expert_ids`: each row names 8 different experts. Within each aligned block of 24 rows no expert is named by more than 16 rows; in every run of 16 consecutive blocks starting at a multiple of 16, one expert is named by exactly 16 rows of every block.
All inputs are finite; a program needn't handle non-finite values.
Results may differ from a plain program's by a relative error of at most 0.012.
Values may be sent and summed in bfloat16 or wider, within the bound.
No kernel may reach another device: no remote copies, remote signals or barrier semaphores. Data moves between devices by JAX's collectives and lax.ppermute only.
A program may use at most 64 MiB of HBM per device.

v0:
```python
import jax
import jax.numpy as jnp
from jax import lax
from jax.sharding import PartitionSpec as P


def on_device(tokens, cotangent, route_weights, expert_ids, w_gate, w_up, w_down):
    tok_count, model_width = tokens.shape
    top_count = expert_ids.shape[1]
    experts = lax.axis_size("expert")
    capacity = tok_count // experts * top_count + min(top_count, tok_count % experts)
    slot_rows = experts * capacity
    named_count = jnp.sum(
        (expert_ids[:, :, None] == jnp.arange(experts, dtype=jnp.int32)).astype(jnp.int32), axis=1
    )
    before = jnp.cumsum(named_count, axis=0) - named_count
    position = jnp.take_along_axis(before, expert_ids, axis=1)
    slot_index = (expert_ids * capacity + position).reshape(-1)
    copies = jnp.broadcast_to(tokens[:, None, :], (tok_count, top_count, model_width)).reshape(
        -1, model_width
    )
    scaled = (
        (route_weights[:, :, None] * cotangent[:, None, :].astype(jnp.float32))
        .astype(jnp.bfloat16)
        .reshape(-1, model_width)
    )
    empty_slots = jnp.zeros((slot_rows, model_width), jnp.bfloat16)
    send_rows = empty_slots.at[slot_index].set(copies).reshape(experts, capacity, model_width)
    send_grads = empty_slots.at[slot_index].set(scaled).reshape(experts, capacity, model_width)
    recv_rows, recv_grads = (
        lax.all_to_all(send_rows, "expert", split_axis=0, concat_axis=0, tiled=True),
        lax.all_to_all(send_grads, "expert", split_axis=0, concat_axis=0, tiled=True),
    )
    flat_rows = recv_rows.reshape(slot_rows, model_width)
    flat_grads = recv_grads.reshape(slot_rows, model_width)
    gate_full, up_full, down_full = (
        lax.all_gather(w_gate[0], "dp", axis=1, tiled=True),
        lax.all_gather(w_up[0], "dp", axis=1, tiled=True),
        lax.all_gather(w_down[0], "dp", axis=1, tiled=True),
    )
    contract_last = (((1,), (1,)), ((), ()))
    gate_value = lax.dot_general(
        flat_rows, gate_full, contract_last, preferred_element_type=jnp.float32
    )
    up_value = lax.dot_general(
        flat_rows, up_full, contract_last, preferred_element_type=jnp.float32
    )
    sigmoid_gate = jax.nn.sigmoid(gate_value)
    active = gate_value * sigmoid_gate
    hidden = (active * up_value).astype(jnp.bfloat16)
    mixed_slots = jnp.dot(hidden, down_full, preferred_element_type=jnp.float32).astype(
        jnp.bfloat16
    )
    d_hidden = lax.dot_general(
        flat_grads, down_full, contract_last, preferred_element_type=jnp.float32
    )
    d_gate = (
        d_hidden * up_value * sigmoid_gate * (1.0 + gate_value * (1.0 - sigmoid_gate))
    ).astype(jnp.bfloat16)
    d_up = (d_hidden * active).astype(jnp.bfloat16)
    input_slots = (
        jnp.dot(d_gate, gate_full, preferred_element_type=jnp.float32)
        + jnp.dot(d_up, up_full, preferred_element_type=jnp.float32)
    ).astype(jnp.bfloat16)
    weight_grads = lax.psum_scatter(
        lax.dot_general(
            flat_rows, d_gate, (((0,), (0,)), ((), ())), preferred_element_type=jnp.float32
        ).astype(jnp.bfloat16),
        "dp",
        scatter_dimension=0,
        tiled=True,
    ).astype(jnp.float32)
    grad_gate = jnp.transpose(weight_grads)[None]
    back_mixed, back_input = (
        lax.all_to_all(
            mixed_slots.reshape(experts, capacity, model_width),
            "expert",
            split_axis=0,
            concat_axis=0,
            tiled=True,
        ),
        lax.all_to_all(
            input_slots.reshape(experts, capacity, model_width),
            "expert",
            split_axis=0,
            concat_axis=0,
            tiled=True,
        ),
    )
    token_mixed = back_mixed.reshape(slot_rows, model_width)[slot_index].reshape(
        tok_count, top_count, model_width
    )
    token_input = back_input.reshape(slot_rows, model_width)[slot_index].reshape(
        tok_count, top_count, model_width
    )
    mixed_part = jnp.sum(route_weights[:, :, None] * token_mixed.astype(jnp.float32), axis=1)
    input_part = jnp.sum(token_input.astype(jnp.float32), axis=1)
    mixed, grad_tokens = (
        lax.psum_scatter(
            mixed_part.astype(jnp.bfloat16), "etp", scatter_dimension=1, tiled=True
        ).astype(jnp.float32),
        lax.psum_scatter(
            input_part.astype(jnp.bfloat16), "etp", scatter_dimension=1, tiled=True
        ).astype(jnp.float32),
    )
    return (mixed.astype(jnp.bfloat16), grad_tokens.astype(jnp.bfloat16), grad_gate)


def solution(mesh):
    in_specs = (
        P(("dp", "expert"), None),
        P(("dp", "expert"), None),
        P(("dp", "expert"), None),
        P(("dp", "expert"), None),
        P("expert", "etp", "dp"),
        P("expert", "etp", "dp"),
        P("expert", "etp", "dp"),
    )
    out_specs = (P(("dp", "expert"), "etp"), P(("dp", "expert"), "etp"), P("expert", "etp", "dp"))
    return jax.shard_map(
        on_device, mesh=mesh, in_specs=in_specs, out_specs=out_specs, check_vma=False
    )
```

profile of v0, /device:TPU:8, one launch (start us, length us, event | category | flops | bytes accessed | tf_op | source)
XLA Modules:
  0.0 312.0 jit_solution(12427213311101825373)
XLA Ops:
  7.2 0.7 all-gather.9.cloned.1.call-update
  8.0 0.7 all-gather.11.cloned.1.call-update
  8.7 0.8 copy.22
  9.4 0.7 convert_reduce_fusion
  10.4 1.6 gather_fusion.2
  12.1 0.1 reshape.88
  12.2 4.4 %scatter_custom_fusion = bf16[256,4096]{1,0:T(8,128)(2,1)} fusion(s32[192]{0:T(256)S(1)} %bitcast.61, bf16[]{:T(256)} %constant.10.clone.1, bf16[24,4096]{1,0:T(8,128)(2,1)S(1)} %copy-done), kind=kCustom, calls=%fused_computation.25 | custom fusion | bytes 2293762 | tf_op jit(solution)/shard_map/scatter | solution.py:28
  16.6 9.5 %all-to-all-start = ((bf16[16,16,4096]{2,1,0:T(8,128)(2,1)}), bf16[16,16,4096]{2,1,0:T(8,128)(2,1)S(1)}, u32[]{:S(2)}, u32[]{:S(2)}) async-start(bf16[16,16,4096]{2,1,0:T(8,128)(2,1)} %bitcast.59), calls=%async_computation | async-start | bytes 4194304 | tf_op jit(solution)/shard_map/all_to_all | solution.py:31
  26.1 0.7 all-gather.7.cloned.1.call-update
  27.0 4.3 %scatter_custom_fusion.1 = bf16[256,4096]{1,0:T(8,128)(2,1)} fusion(s32[192]{0:T(256)S(1)} %bitcast.62, f32[24,4096]{1,0:T(8,128)S(1)} %convert_element_type.51, f32[192]{0:T(256)S(1)} %mul.59, bf16[]{:T(256)} %constant.10.clone.1), kind=kCustom, calls=%fused_computation.23 | custom fusion | flops 1572864 | bytes 2491394 | tf_op jit(solution)/shard_map/scatter | solution.py:29
  31.3 42.1 %all-to-all-done = bf16[16,16,4096]{2,1,0:T(8,128)(2,1)S(1)} async-done(((bf16[16,16,4096]{2,1,0:T(8,128)(2,1)}), bf16[16,16,4096]{2,1,0:T(8,128)(2,1)S(1)}, u32[]{:S(2)}, u32[]{:S(2)}) %all-to-all-start) | async-done | bytes 2097184 | tf_op jit(solution)/shard_map/all_to_all | solution.py:31
  73.4 6.6 %all-to-all-start.2 = ((bf16[16,16,4096]{2,1,0:T(8,128)(2,1)}), bf16[16,16,4096]{2,1,0:T(8,128)(2,1)}, u32[]{:S(2)}, u32[]{:S(2)}) async-start(bf16[16,16,4096]{2,1,0:T(8,128)(2,1)} %bitcast.60), calls=%async_computation.3 | async-start | bytes 4194304 | tf_op jit(solution)/shard_map/all_to_all | solution.py:32
  80.0 3.9 %fusion.7 = f32[256,384]{1,0:T(8,128)} fusion(bf16[256,4096]{1,0:T(8,128)(2,1)S(1)} %bitcast.54, bf16[1,384,4096]{2,1,0:T(8,128)(2,1)} %all-gather.9.cloned.1.call-done), kind=kOutput, calls=%fused_computation.17 | convolution fusion | flops 805306368 | bytes 5636096 | tf_op jit(solution)/shard_map/dot_general | solution.py:45
  83.9 43.6 %all-to-all-done.2 = bf16[16,16,4096]{2,1,0:T(8,128)(2,1)} async-done(((bf16[16,16,4096]{2,1,0:T(8,128)(2,1)}), bf16[16,16,4096]{2,1,0:T(8,128)(2,1)}, u32[]{:S(2)}, u32[]{:S(2)}) %all-to-all-start.2) | async-done | bytes 2097184 | tf_op jit(solution)/shard_map/all_to_all | solution.py:32
  127.5 3.8 %fusion.3 = f32[256,384]{1,0:T(8,128)S(1)} fusion(bf16[256,4096]{1,0:T(8,128)(2,1)} %bitcast.13, bf16[1,384,4096]{2,1,0:T(8,128)(2,1)} %all-gather.11.cloned.1.call-done), kind=kOutput, calls=%fused_computation.13 | convolution fusion | flops 805306368 | bytes 5636096 | tf_op jit(solution)/shard_map/dot_general | solution.py:54
  131.3 29.1 %all-gather.7.cloned.1.call-done = bf16[1,384,4096]{2,1,0:T(8,128)(2,1)} async-done(((bf16[1,384,512]{2,1,0:T(8,128)(2,1)}), bf16[1,384,4096]{2,1,0:T(8,128)(2,1)}) %all-gather.7.cloned.1.call-update) | async-done | bytes 3145744 | tf_op jit(solution)/shard_map/all_gather | solution.py:37
  160.4 3.4 %multiply_convert_fusion.1 = (bf16[256,384]{1,0:T(8,128)(2,1)S(1)}, f32[256,384]{1,0:T(8,128)S(1)}) fusion(f32[256,384]{1,0:T(8,128)S(1)} %fusion.3, f32[256,384]{1,0:T(8,128)} %fusion.7, bf16[256,4096]{1,0:T(8,128)(2,1)S(1)} %bitcast.55, bf16[1,384,4096]{2,1,0:T(8,128)(2,1)} %all-gather.7.cloned.1.call-done), kind=kOutput, calls=%fused_computation.34 | convolution fusion | flops 806289408 | bytes 6619136 | tf_op jit(solution)/shard_map/dot_general | solution.py:42
  163.8 2.6 convolution_convert_fusion.1
  166.4 7.3 %all-to-all-start.1 = ((bf16[16,16,4096]{2,1,0:T(8,128)(2,1)}), bf16[16,16,4096]{2,1,0:T(8,128)(2,1)S(1)}, u32[]{:S(2)}, u32[]{:S(2)}) async-start(bf16[16,16,4096]{2,1,0:T(8,128)(2,1)} %bitcast.58), calls=%async_computation.1 | async-start | bytes 4194304 | tf_op jit(solution)/shard_map/all_to_all | solution.py:75
  173.8 4.6 %convolution_convert_fusion = bf16[4096,384]{1,0:T(8,128)(2,1)} fusion(bf16[256,4096]{1,0:T(8,128)(2,1)} %bitcast.56, bf16[256,384]{1,0:T(8,128)(2,1)S(1)} %get-tuple-element.12), kind=kOutput, calls=%fused_computation.5 | convolution fusion | flops 806879232 | bytes 5439488 | tf_op jit(solution)/shard_map/dot_general | solution.py:66
  178.4 3.3 %fusion.9 = f32[256,4096]{1,0:T(8,128)S(1)} fusion(bf16[256,384]{1,0:T(8,128)(2,1)S(1)} %get-tuple-element.12, bf16[1,384,4096]{2,1,0:T(8,128)(2,1)} %all-gather.7.cloned.1.call-done), kind=kOutput, calls=%fused_computation.19 | convolution fusion | flops 805306368 | bytes 7536640 | tf_op jit(solution)/shard_map/dot_general | solution.py:62
  181.7 2.7 fusion
  184.3 36.8 %all-to-all-done.1 = bf16[16,16,4096]{2,1,0:T(8,128)(2,1)S(1)} async-done(((bf16[16,16,4096]{2,1,0:T(8,128)(2,1)}), bf16[16,16,4096]{2,1,0:T(8,128)(2,1)S(1)}, u32[]{:S(2)}, u32[]{:S(2)}) %all-to-all-start.1) | async-done | bytes 2097184 | tf_op jit(solution)/shard_map/all_to_all | solution.py:75
  221.1 6.5 %all-to-all-start.3 = ((bf16[16,16,4096]{2,1,0:T(8,128)(2,1)}), bf16[16,16,4096]{2,1,0:T(8,128)(2,1)}, u32[]{:S(2)}, u32[]{:S(2)}) async-start(bf16[16,16,4096]{2,1,0:T(8,128)(2,1)} %bitcast.57), calls=%async_computation.4 | async-start | bytes 4194304 | tf_op jit(solution)/shard_map/all_to_all | solution.py:82
  227.7 2.7 gather_fusion
  230.4 3.3 %fusion.1 = bf16[24,4096]{1,0:T(8,128)(2,1)} fusion(bf16[192,4096]{1,0:T(8,128)(2,1)} %gather_fusion, f32[24,8]{1,0:T(8,128)S(1)} %copy.21), kind=kLoop, calls=%fused_computation.10 | loop fusion | flops 2260992 | bytes 1770240 | tf_op jit(solution)/shard_map/reduce_sum | solution.py:96
  233.8 41.3 %all-to-all-done.3 = bf16[16,16,4096]{2,1,0:T(8,128)(2,1)} async-done(((bf16[16,16,4096]{2,1,0:T(8,128)(2,1)}), bf16[16,16,4096]{2,1,0:T(8,128)(2,1)}, u32[]{:S(2)}, u32[]{:S(2)}) %all-to-all-start.3) | async-done | bytes 2097184 | tf_op jit(solution)/shard_map/all_to_all | solution.py:82
  275.1 4.9 %gather_fusion.1 = bf16[192,4096]{1,0:T(8,128)(2,1)S(1)} fusion(bf16[256,4096]{1,0:T(8,128)(2,1)} %bitcast.15, s32[1024]{0:T(1024)S(1)} %pad_clamp_fusion), kind=kCustom, calls=%fused_computation.1 | custom fusion | bytes 3146496 | tf_op jit(solution)/shard_map/gather | solution.py:93
  280.1 1.7 bitcast_reduce_fusion
  281.8 1.0 convert_bitcast_fusion
  282.9 1.1 copy.29
  284.0 21.1 %reduce-scatter.6.cloned.1.call-done = bf16[24,1024]{1,0:T(8,128)(2,1)} async-done(((bf16[24,4096]{1,0:T(8,128)(2,1)}), bf16[24,1024]{1,0:T(8,128)(2,1)}) %reduce-scatter.6.cloned.1.call-update) | async-done | bytes 49168 | tf_op jit(solution)/shard_map/reduce_scatter | solution.py:102
  (39 shorter events, 0.9 us)
Async XLA Ops:
  7.2 5.0 %copy-start = (bf16[24,4096]{1,0:T(8,128)(2,1)S(1)}, bf16[24,4096]{1,0:T(8,128)(2,1)}, u32[]{:S(2)}) copy-start(bf16[24,4096]{1,0:T(8,128)(2,1)} %param.7) | copy-start | bytes 589828
  7.2 72.8 %all-gather.9.cloned.1.call-start = ((), (), s32[]{:S(2)}) async-start(), calls=%async_computation.11 | async-start | bytes 3538944 | tf_op jit(solution)/shard_map/all_gather | solution.py:38
  7.9 119.6 %all-gather.11.cloned.1.call-start = ((), (), s32[]{:S(2)}) async-start(), calls=%async_computation.12 | async-start | bytes 3538944 | tf_op jit(solution)/shard_map/all_gather | solution.py:39
  16.6 10.2 %copy-start.5 = (bf16[24,4096]{1,0:T(8,128)(2,1)S(1)}, bf16[24,4096]{1,0:T(8,128)(2,1)}, u32[]{:S(2)}) copy-start(bf16[24,4096]{1,0:T(8,128)(2,1)} %param.8) | copy-start | bytes 589828
  16.6 10.3 %copy-start.6 = (f32[24,8]{0,1:T(8,128)S(1)}, f32[24,8]{0,1:T(8,128)}, u32[]{:S(2)}) copy-start(f32[24,8]{0,1:T(8,128)} %param.9) | copy-start | bytes 2308
  16.6 56.9 %all-to-all-start = ((bf16[16,16,4096]{2,1,0:T(8,128)(2,1)}), bf16[16,16,4096]{2,1,0:T(8,128)(2,1)S(1)}, u32[]{:S(2)}, u32[]{:S(2)}) async-start(bf16[16,16,4096]{2,1,0:T(8,128)(2,1)} %bitcast.59), calls=%async_computation | async-start | bytes 4194304 | tf_op jit(solution)/shard_map/all_to_all | solution.py:31
  26.0 134.3 %all-gather.7.cloned.1.call-start = ((), (), s32[]{:S(2)}) async-start(), calls=%async_computation.10 | async-start | bytes 3538944 | tf_op jit(solution)/shard_map/all_gather | solution.py:37
  73.4 86.9 %copy-start.1 = (bf16[16,16,4096]{2,1,0:T(8,128)(2,1)}, bf16[16,16,4096]{2,1,0:T(8,128)(2,1)S(1)}, u32[]{:S(2)}) copy-start(bf16[16,16,4096]{2,1,0:T(8,128)(2,1)S(1)} %all-to-all-done) | copy-start | bytes 6291460
  73.4 54.1 %all-to-all-start.2 = ((bf16[16,16,4096]{2,1,0:T(8,128)(2,1)}), bf16[16,16,4096]{2,1,0:T(8,128)(2,1)}, u32[]{:S(2)}, u32[]{:S(2)}) async-start(bf16[16,16,4096]{2,1,0:T(8,128)(2,1)} %bitcast.60), calls=%async_computation.3 | async-start | bytes 4194304 | tf_op jit(solution)/shard_map/all_to_all | solution.py:32
  160.4 3.4 %copy-start.2 = (bf16[1,384,4096]{2,1,0:T(8,128)(2,1)S(1)}, bf16[1,384,4096]{2,1,0:T(8,128)(2,1)}, u32[]{:S(2)}) copy-start(bf16[1,384,4096]{2,1,0:T(8,128)(2,1)} %all-gather.11.cloned.1.call-done) | copy-start | bytes 9437188
  160.4 3.5 %copy-start.4 = (f32[256,384]{1,0:T(8,128)S(1)}, f32[256,384]{1,0:T(8,128)}, u32[]{:S(2)}) copy-start(f32[256,384]{1,0:T(8,128)} %fusion.7) | copy-start | bytes 1179652
  166.4 54.7 %all-to-all-start.1 = ((bf16[16,16,4096]{2,1,0:T(8,128)(2,1)}), bf16[16,16,4096]{2,1,0:T(8,128)(2,1)S(1)}, u32[]{:S(2)}, u32[]{:S(2)}) async-start(bf16[16,16,4096]{2,1,0:T(8,128)(2,1)} %bitcast.58), calls=%async_computation.1 | async-start | bytes 4194304 | tf_op jit(solution)/shard_map/all_to_all | solution.py:75
  173.7 108.1 %reduce-scatter.8.cloned.1.call-start = ((), (), s32[]{:S(2)}) async-start(), calls=%async_computation.9 | async-start | bytes 3538944 | tf_op jit(solution)/shard_map/reduce_scatter | solution.py:65
  178.4 3.3 %copy-start.3 = (bf16[1,384,4096]{2,1,0:T(8,128)(2,1)S(1)}, bf16[1,384,4096]{2,1,0:T(8,128)(2,1)}, u32[]{:S(2)}) copy-start(bf16[1,384,4096]{2,1,0:T(8,128)(2,1)} %all-gather.9.cloned.1.call-done) | copy-start | bytes 9437188
  221.1 54.0 %all-to-all-start.3 = ((bf16[16,16,4096]{2,1,0:T(8,128)(2,1)}), bf16[16,16,4096]{2,1,0:T(8,128)(2,1)}, u32[]{:S(2)}, u32[]{:S(2)}) async-start(bf16[16,16,4096]{2,1,0:T(8,128)(2,1)} %bitcast.57), calls=%async_computation.4 | async-start | bytes 4194304 | tf_op jit(solution)/shard_map/all_to_all | solution.py:82
  227.7 56.4 %reduce-scatter.4.cloned.1.call-start = ((), (), s32[]{:S(2)}) async-start(), calls=%async_computation.7 | async-start | bytes 245760 | tf_op jit(solution)/shard_map/reduce_scatter | solution.py:99
  233.8 71.4 %reduce-scatter.6.cloned.1.call-start = ((), (), s32[]{:S(2)}) async-start(), calls=%async_computation.8 | async-start | bytes 245760 | tf_op jit(solution)/shard_map/reduce_scatter | solution.py:102
Sparse Core Ops, SparseCore 0:
  10.1 52.9 all-gather.8
  65.2 46.4 all-gather.10
  113.8 46.4 all-gather.6
  178.5 48.1 reduce-scatter.7
  233.9 23.8 reduce-scatter.3
  281.9 23.1 reduce-scatter.5
where the time goes:
time: 313 us; the launch traced here: 312 us
  waiting for transfers between devices  216 us (69%)
  starting transfers between devices  30.1 us (10%)
  matrix products  24.2 us (8%)
  local copies, waits for them, and re-layouts  16.1 us (5%)
  between operations  14.3 us (5%)
  other arithmetic  11.2 us (4%)
    all_to_all x1, waiting for transfers between devices, on_device(): lax.all_to_all(send_grads, 'expert', split_axis=0, concat_axis=0, tiled=T...  43.6 us
    all_to_all x1, waiting for transfers between devices, on_device(): lax.all_to_all(send_rows, 'expert', split_axis=0, concat_axis=0, tiled=True)  42.1 us
    all_to_all x1, waiting for transfers between devices, on_device(): lax.all_to_all(input_slots.reshape(experts, capacity, model_width), 'expe...  41.3 us
    all_to_all x1, waiting for transfers between devices, on_device(): lax.all_to_all(mixed_slots.reshape(experts, capacity, model_width), 'expe...  36.8 us
    all_gather x1, waiting for transfers between devices, on_device(): lax.all_gather(w_gate[0], 'dp', axis=1, tiled=True)  29.1 us
    reduce_scatter x1, waiting for transfers between devices, on_device(): lax.psum_scatter(input_part.astype(jnp.bfloat16), 'etp', scatter_dimensio...  21.1 us
    all_to_all x1, starting transfers between devices, on_device(): lax.all_to_all(send_rows, 'expert', split_axis=0, concat_axis=0, tiled=True)  9.47 us
    all_to_all x1, starting transfers between devices, on_device(): lax.all_to_all(mixed_slots.reshape(experts, capacity, model_width), 'expe...  7.29 us
  transfers between devices with their start and end apart: 10, of which 6 were waited for; matrix products, arithmetic and copies ran while one was open for 15% of the time, Pallas kernels for 0%

commit v1 on v0

--- a/solution.py
+++ b/solution.py
@@ -34,7 +34,9 @@
     flat_rows = recv_rows.reshape(slot_rows, model_width)
     flat_grads = recv_grads.reshape(slot_rows, model_width)
     gate_full, up_full, down_full = (
-        lax.all_gather(w_gate[0], "dp", axis=1, tiled=True),
+        jnp.concatenate(
+            lax.all_to_all(jnp.stack([w_gate[0]] * lax.axis_size("dp")), "dp", 0, 0), axis=1
+        ),
         lax.all_gather(w_up[0], "dp", axis=1, tiled=True),
         lax.all_gather(w_down[0], "dp", axis=1, tiled=True),
     )

time: 313 us -> 360 us (1.15)
  waiting for transfers between devices: 216 us -> 254 us
  starting transfers between devices: 30.1 us -> 37.7 us
    all_to_all x0 -> x1, waiting for transfers between devices: none -> 66.9 us  [on_device(): lax.all_to_all(jnp.stack([w_gate[0]] * lax.axis_size('dp')), 'dp', 0, 0)]
    all_gather x1 -> x0, waiting for transfers between devices: 29.1 us -> none  [on_device(): lax.all_gather(w_gate[0], 'dp', axis=1, tiled=True)]
    all_to_all x0 -> x1, starting transfers between devices: none -> 8.51 us  [on_device(): lax.all_to_all(jnp.stack([w_gate[0]] * lax.axis_size('dp')), 'dp', 0, 0)]
  transfers between devices with their start and end apart: 10 -> 10, of which waited for: 6 -> 6; matrix products, arithmetic and copies ran while one was open for 15% -> 11% of each run, Pallas kernels for 0% -> 0%
where the time goes in v1:
time: 360 us
  waiting for transfers between devices  254 us (71%)
  starting transfers between devices  37.7 us (10%)
  matrix products  24.3 us (7%)
  local copies, waits for them, and re-layouts  18.1 us (5%)
  between operations  14 us (4%)
  other arithmetic  11.3 us (3%)
    all_to_all x1, waiting for transfers between devices, on_device(): lax.all_to_all(jnp.stack([w_gate[0]] * lax.axis_size('dp')), 'dp', 0, 0)  66.9 us
    all_to_all x1, waiting for transfers between devices, on_device(): lax.all_to_all(send_grads, 'expert', split_axis=0, concat_axis=0, tiled=T...  46.5 us
    all_to_all x1, waiting for transfers between devices, on_device(): lax.all_to_all(send_rows, 'expert', split_axis=0, concat_axis=0, tiled=True)  42.1 us
    all_to_all x1, waiting for transfers between devices, on_device(): lax.all_to_all(input_slots.reshape(experts, capacity, model_width), 'expe...  41.1 us
    all_to_all x1, waiting for transfers between devices, on_device(): lax.all_to_all(mixed_slots.reshape(experts, capacity, model_width), 'expe...  36.7 us
    reduce_scatter x1, waiting for transfers between devices, on_device(): lax.psum_scatter(input_part.astype(jnp.bfloat16), 'etp', scatter_dimensio...  19.3 us
    all_to_all x1, starting transfers between devices, on_device(): lax.all_to_all(send_rows, 'expert', split_axis=0, concat_axis=0, tiled=True)  9.47 us
    all_to_all x1, starting transfers between devices, on_device(): lax.all_to_all(jnp.stack([w_gate[0]] * lax.axis_size('dp')), 'dp', 0, 0)  8.51 us
  transfers between devices with their start and end apart: 10, of which 6 were waited for; matrix products, arithmetic and copies ran while one was open for 11% of the time, Pallas kernels for 0%

profile of v1, /device:TPU:8, one launch (start us, length us, event | category | flops | bytes accessed | tf_op | source)
XLA Modules:
  0.0 359.5 jit_solution(239687500509632660)
XLA Ops:
  7.2 0.7 convert_reduce_fusion
  7.9 0.8 copy.23
  8.9 1.6 gather_fusion.2
  10.7 4.3 %scatter_custom_fusion = bf16[256,4096]{1,0:T(8,128)(2,1)} fusion(s32[192]{0:T(256)S(1)} %bitcast.61, bf16[]{:T(256)} %constant.10.clone.1, bf16[24,4096]{1,0:T(8,128)(2,1)S(1)} %copy-done), kind=kCustom, calls=%fused_computation.21 | custom fusion | bytes 2293762 | tf_op jit(solution)/shard_map/scatter | solution.py:28
  15.0 9.5 %all-to-all-start = ((bf16[16,16,4096]{2,1,0:T(8,128)(2,1)}), bf16[16,16,4096]{2,1,0:T(8,128)(2,1)S(1)}, u32[]{:S(2)}, u32[]{:S(2)}) async-start(bf16[16,16,4096]{2,1,0:T(8,128)(2,1)} %bitcast.59), calls=%async_computation | async-start | bytes 4194304 | tf_op jit(solution)/shard_map/all_to_all | solution.py:31
  24.6 0.7 all-gather.5.cloned.1.call-update
  25.5 4.4 %scatter_custom_fusion.1 = bf16[256,4096]{1,0:T(8,128)(2,1)} fusion(s32[192]{0:T(256)S(1)} %bitcast.62, f32[24,4096]{1,0:T(8,128)S(1)} %convert_element_type.51, f32[192]{0:T(256)S(1)} %mul.59, bf16[]{:T(256)} %constant.10.clone.1), kind=kCustom, calls=%fused_computation.19 | custom fusion | flops 1572864 | bytes 2491394 | tf_op jit(solution)/shard_map/scatter | solution.py:29
  29.8 42.1 %all-to-all-done = bf16[16,16,4096]{2,1,0:T(8,128)(2,1)S(1)} async-done(((bf16[16,16,4096]{2,1,0:T(8,128)(2,1)}), bf16[16,16,4096]{2,1,0:T(8,128)(2,1)S(1)}, u32[]{:S(2)}, u32[]{:S(2)}) %all-to-all-start) | async-done | bytes 2097184 | tf_op jit(solution)/shard_map/all_to_all | solution.py:31
  71.9 6.7 %all-to-all-start.3 = ((bf16[16,16,4096]{2,1,0:T(8,128)(2,1)}), bf16[16,16,4096]{2,1,0:T(8,128)(2,1)}, u32[]{:S(2)}, u32[]{:S(2)}) async-start(bf16[16,16,4096]{2,1,0:T(8,128)(2,1)} %bitcast.58), calls=%async_computation.4 | async-start | bytes 4194304 | tf_op jit(solution)/shard_map/all_to_all | solution.py:32
  78.7 0.7 all-gather.7.cloned.1.call-update
  79.6 46.5 %all-to-all-done.3 = bf16[16,16,4096]{2,1,0:T(8,128)(2,1)} async-done(((bf16[16,16,4096]{2,1,0:T(8,128)(2,1)}), bf16[16,16,4096]{2,1,0:T(8,128)(2,1)}, u32[]{:S(2)}, u32[]{:S(2)}) %all-to-all-start.3) | async-done | bytes 2097184 | tf_op jit(solution)/shard_map/all_to_all | solution.py:32
  126.1 1.9 stack.3
  128.0 8.5 %all-to-all-start.1 = ((bf16[8,384,512]{1,2,0:T(8,128)(2,1)}), bf16[8,384,512]{1,2,0:T(8,128)(2,1)}, u32[]{:S(2)}, u32[]{:S(2)}) async-start(bf16[8,384,512]{1,2,0:T(8,128)(2,1)} %stack.3), calls=%async_computation.1 | async-start | bytes 6291456 | tf_op jit(solution)/shard_map/all_to_all | solution.py:38
  136.6 3.9 %fusion.7 = f32[256,384]{1,0:T(8,128)} fusion(bf16[256,4096]{1,0:T(8,128)(2,1)S(1)} %bitcast.53, bf16[1,384,4096]{2,1,0:T(8,128)(2,1)} %all-gather.5.cloned.1.call-done), kind=kOutput, calls=%fused_computation.17 | convolution fusion | flops 805306368 | bytes 5636096 | tf_op jit(solution)/shard_map/dot_general | solution.py:47
  140.5 3.8 %fusion.3 = f32[256,384]{1,0:T(8,128)S(1)} fusion(bf16[256,4096]{1,0:T(8,128)(2,1)} %bitcast.15, bf16[1,384,4096]{2,1,0:T(8,128)(2,1)} %all-gather.7.cloned.1.call-done), kind=kOutput, calls=%fused_computation.13 | convolution fusion | flops 805306368 | bytes 5636096 | tf_op jit(solution)/shard_map/dot_general | solution.py:56
  144.3 66.9 %all-to-all-done.1 = bf16[8,384,512]{1,2,0:T(8,128)(2,1)} async-done(((bf16[8,384,512]{1,2,0:T(8,128)(2,1)}), bf16[8,384,512]{1,2,0:T(8,128)(2,1)}, u32[]{:S(2)}, u32[]{:S(2)}) %all-to-all-start.1) | async-done | bytes 3145760 | tf_op jit(solution)/shard_map/all_to_all | solution.py:38
  211.2 3.4 multiply_convert_fusion.1
  214.6 2.6 convolution_convert_fusion.1
  217.2 6.1 %all-to-all-start.2 = ((bf16[16,16,4096]{2,1,0:T(8,128)(2,1)}), bf16[16,16,4096]{2,1,0:T(8,128)(2,1)S(1)}, u32[]{:S(2)}, u32[]{:S(2)}) async-start(bf16[16,16,4096]{2,1,0:T(8,128)(2,1)} %bitcast.57), calls=%async_computation.2 | async-start | bytes 4194304 | tf_op jit(solution)/shard_map/all_to_all | solution.py:77
  223.4 4.6 %convolution_convert_fusion = bf16[4096,384]{1,0:T(8,128)(2,1)} fusion(bf16[256,4096]{1,0:T(8,128)(2,1)} %bitcast.55, bf16[256,384]{1,0:T(8,128)(2,1)S(1)} %get-tuple-element.12), kind=kOutput, calls=%fused_computation.5 | convolution fusion | flops 806879232 | bytes 5439488 | tf_op jit(solution)/shard_map/dot_general | solution.py:68
  228.0 3.3 fusion.23
  231.3 2.7 fusion
  233.9 36.7 %all-to-all-done.2 = bf16[16,16,4096]{2,1,0:T(8,128)(2,1)S(1)} async-done(((bf16[16,16,4096]{2,1,0:T(8,128)(2,1)}), bf16[16,16,4096]{2,1,0:T(8,128)(2,1)S(1)}, u32[]{:S(2)}, u32[]{:S(2)}) %all-to-all-start.2) | async-done | bytes 2097184 | tf_op jit(solution)/shard_map/all_to_all | solution.py:77
  270.7 6.5 %all-to-all-start.4 = ((bf16[16,16,4096]{2,1,0:T(8,128)(2,1)}), bf16[16,16,4096]{2,1,0:T(8,128)(2,1)}, u32[]{:S(2)}, u32[]{:S(2)}) async-start(bf16[16,16,4096]{2,1,0:T(8,128)(2,1)} %bitcast.56), calls=%async_computation.5 | async-start | bytes 4194304 | tf_op jit(solution)/shard_map/all_to_all | solution.py:84
  277.3 2.7 gather_fusion
  280.0 3.3 fusion.1
  283.6 41.1 %all-to-all-done.4 = bf16[16,16,4096]{2,1,0:T(8,128)(2,1)} async-done(((bf16[16,16,4096]{2,1,0:T(8,128)(2,1)}), bf16[16,16,4096]{2,1,0:T(8,128)(2,1)}, u32[]{:S(2)}, u32[]{:S(2)}) %all-to-all-start.4) | async-done | bytes 2097184 | tf_op jit(solution)/shard_map/all_to_all | solution.py:84
  324.7 4.9 %gather_fusion.1 = bf16[192,4096]{1,0:T(8,128)(2,1)S(1)} fusion(bf16[256,4096]{1,0:T(8,128)(2,1)} %bitcast.18, s32[1024]{0:T(1024)S(1)} %pad_clamp_fusion), kind=kCustom, calls=%fused_computation.1 | custom fusion | bytes 3146496 | tf_op jit(solution)/shard_map/gather | solution.py:95
  329.6 1.7 bitcast_reduce_fusion
  331.4 1.0 convert_bitcast_fusion
  332.5 1.1 copy.31
  333.6 19.3 %reduce-scatter.6.cloned.1.call-done = bf16[24,1024]{1,0:T(8,128)(2,1)} async-done(((bf16[24,4096]{1,0:T(8,128)(2,1)}), bf16[24,1024]{1,0:T(8,128)(2,1)}) %reduce-scatter.6.cloned.1.call-update) | async-done | bytes 49168 | tf_op jit(solution)/shard_map/reduce_scatter | solution.py:104
  (42 shorter events, 1.3 us)
Async XLA Ops:
  7.2 3.6 copy-start
  15.0 10.2 %copy-start.6 = (bf16[24,4096]{1,0:T(8,128)(2,1)S(1)}, bf16[24,4096]{1,0:T(8,128)(2,1)}, u32[]{:S(2)}) copy-start(bf16[24,4096]{1,0:T(8,128)(2,1)} %param.8) | copy-start | bytes 589828
  15.0 10.3 %copy-start.7 = (f32[24,8]{0,1:T(8,128)S(1)}, f32[24,8]{0,1:T(8,128)}, u32[]{:S(2)}) copy-start(f32[24,8]{0,1:T(8,128)} %param.9) | copy-start | bytes 2308
  15.0 56.9 %all-to-all-start = ((bf16[16,16,4096]{2,1,0:T(8,128)(2,1)}), bf16[16,16,4096]{2,1,0:T(8,128)(2,1)S(1)}, u32[]{:S(2)}, u32[]{:S(2)}) async-start(bf16[16,16,4096]{2,1,0:T(8,128)(2,1)} %bitcast.59), calls=%async_computation | async-start | bytes 4194304 | tf_op jit(solution)/shard_map/all_to_all | solution.py:31
  24.5 112.0 %all-gather.5.cloned.1.call-start = ((), (), s32[]{:S(2)}) async-start(), calls=%async_computation.11 | async-start | bytes 3538944 | tf_op jit(solution)/shard_map/all_gather | solution.py:40
  71.9 139.3 %copy-start.1 = (bf16[16,16,4096]{2,1,0:T(8,128)(2,1)}, bf16[16,16,4096]{2,1,0:T(8,128)(2,1)S(1)}, u32[]{:S(2)}) copy-start(bf16[16,16,4096]{2,1,0:T(8,128)(2,1)S(1)} %all-to-all-done) | copy-start | bytes 6291460
  71.9 7.5 %copy-start.5 = (bf16[1,384,512]{2,1,0:T(8,128)(2,1)S(1)}, bf16[1,384,512]{2,1,0:T(8,128)(2,1)}, u32[]{:S(2)}) copy-start(bf16[1,384,512]{2,1,0:T(8,128)(2,1)} %param.11) | copy-start | bytes 1179652
  71.9 54.2 %all-to-all-start.3 = ((bf16[16,16,4096]{2,1,0:T(8,128)(2,1)}), bf16[16,16,4096]{2,1,0:T(8,128)(2,1)}, u32[]{:S(2)}, u32[]{:S(2)}) async-start(bf16[16,16,4096]{2,1,0:T(8,128)(2,1)} %bitcast.58), calls=%async_computation.4 | async-start | bytes 4194304 | tf_op jit(solution)/shard_map/all_to_all | solution.py:32
  78.6 61.9 %all-gather.7.cloned.1.call-start = ((), (), s32[]{:S(2)}) async-start(), calls=%async_computation.12 | async-start | bytes 3538944 | tf_op jit(solution)/shard_map/all_gather | solution.py:41
  128.0 83.1 %all-to-all-start.1 = ((bf16[8,384,512]{1,2,0:T(8,128)(2,1)}), bf16[8,384,512]{1,2,0:T(8,128)(2,1)}, u32[]{:S(2)}, u32[]{:S(2)}) async-start(bf16[8,384,512]{1,2,0:T(8,128)(2,1)} %stack.3), calls=%async_computation.1 | async-start | bytes 6291456 | tf_op jit(solution)/shard_map/all_to_all | solution.py:38
  211.2 3.4 copy-start.2
  211.2 3.5 copy-start.4
  217.2 53.5 %all-to-all-start.2 = ((bf16[16,16,4096]{2,1,0:T(8,128)(2,1)}), bf16[16,16,4096]{2,1,0:T(8,128)(2,1)S(1)}, u32[]{:S(2)}, u32[]{:S(2)}) async-start(bf16[16,16,4096]{2,1,0:T(8,128)(2,1)} %bitcast.57), calls=%async_computation.2 | async-start | bytes 4194304 | tf_op jit(solution)/shard_map/all_to_all | solution.py:77
  223.3 108.1 %reduce-scatter.8.cloned.1.call-start = ((), (), s32[]{:S(2)}) async-start(), calls=%async_computation.10 | async-start | bytes 3538944 | tf_op jit(solution)/shard_map/reduce_scatter | solution.py:67
  227.9 3.3 copy-start.3
  270.7 54.0 %all-to-all-start.4 = ((bf16[16,16,4096]{2,1,0:T(8,128)(2,1)}), bf16[16,16,4096]{2,1,0:T(8,128)(2,1)}, u32[]{:S(2)}, u32[]{:S(2)}) async-start(bf16[16,16,4096]{2,1,0:T(8,128)(2,1)} %bitcast.56), calls=%async_computation.5 | async-start | bytes 4194304 | tf_op jit(solution)/shard_map/all_to_all | solution.py:84
  277.2 56.4 %reduce-scatter.4.cloned.1.call-start = ((), (), s32[]{:S(2)}) async-start(), calls=%async_computation.8 | async-start | bytes 245760 | tf_op jit(solution)/shard_map/reduce_scatter | solution.py:101
  283.3 69.6 %reduce-scatter.6.cloned.1.call-start = ((), (), s32[]{:S(2)}) async-start(), calls=%async_computation.9 | async-start | bytes 245760 | tf_op jit(solution)/shard_map/reduce_scatter | solution.py:104
Sparse Core Ops, SparseCore 0:
  27.4 50.8 all-gather.4
  81.5 50.8 all-gather.6
  228.1 46.3 reduce-scatter.7
  283.5 22.1 reduce-scatter.3
  331.5 21.4 reduce-scatter.5
